TPU v7x, 256 devices: a whole 4x4x8 slice. The times are simulated.
256 devices in a mesh: dp: 4 (over y), expert: 64 (over z, x, core).
Axes of the slice: x: 4, y: 4, z: 8, core: 2. Of those that a mesh axis runs over, the one named last changes fastest.
Arguments:
- hidden_states: bfloat16 [1024, 4, 4096], P('expert'), may hold values from -6 to 6
- routes: int32 [1024, 4, 8], P('expert'), may hold values from 0 to 63, all different within a row; in each aligned block of 64 rows (0 to 63, 64 to 127, ..., all dimensions but the last counted through in order) at most 16 rows name the same one
- route_weight: float32 [1024, 4, 8], P('expert'), may hold values from 0.05 to 1
- finish_step: int32 [1024], P('expert'), may hold values from 1 to 4
- group_keep: int32 [64], P('expert'), may hold values from 0 to 1
- dest_slot: int32 [1024], P('expert'), may hold values from 0 to 1023, as said below
- w_gate: bfloat16 [64, 4096, 1536], P('expert', None, 'dp'), may hold values from -0.09375 to 0.09375
- w_up: bfloat16 [64, 4096, 1536], P('expert', None, 'dp'), may hold values from -0.09375 to 0.09375
- w_down: bfloat16 [64, 1536, 4096], P('expert', 'dp'), may hold values from -0.15625 to 0.15625
Outputs:
- trainer_rows: bfloat16 [1024, 4, 4096], P(('dp', 'expert'))
Inputs may be any that keep to these rules, and one draw needn't show every extreme that they name: `routes`: in the 64 row-steps of one prompt group (rows g * 16 to (g + 1) * 16 - 1, all steps), no expert is named more than 16 times, a bound that some block reaches; a row names 8 different experts at each step. dest_slot is a permutation of the slots; row r of group g = r // 16 goes to a slot (d * 64 + g) * 4 + i with 0 <= d < 4 and 0 <= i < 4.
All inputs are finite; a program needn't handle non-finite values.
Results may differ from a plain program's by a relative error of at most 0.0049.
Values may be sent and summed in bfloat16 or wider, within the bound.
No kernel may reach another device: no remote copies, remote signals or barrier semaphores. Data moves between devices by JAX's collectives and lax.ppermute only.
A program may use at most 128 MiB of HBM per device.

v0:
```python
import jax
import jax.numpy as jnp
from jax import lax
from jax.sharding import PartitionSpec as P

MOST_BASE = 16


def exchange_gather(matrix, replica, replica_count):
    width = matrix.shape[1] // replica_count
    pieces = [lax.dynamic_slice_in_dim(matrix, replica * width, width, axis=1)]
    for shift in range(1, replica_count):
        start = (replica + shift) % replica_count * width
        outgoing = lax.dynamic_slice_in_dim(matrix, start, width, axis=1)
        pairs = [(i, (i + shift) % replica_count) for i in range(replica_count)]
        pieces.append(lax.ppermute(outgoing, "dp", pairs))
    return pieces


def exchange_all(block, replica_count):
    pieces = [block]
    for shift in range(1, replica_count):
        pairs = [(i, (i + shift) % replica_count) for i in range(replica_count)]
        pieces.append(lax.ppermute(block, "dp", pairs))
    return jnp.stack(pieces, axis=0)


def body(
    hidden_states, routes, route_weight, finish_step, group_keep, dest_slot, w_gate, w_up, w_down
):
    expert_count = lax.axis_size("expert")
    replica_count = lax.axis_size("dp")
    replica = lax.axis_index("dp")
    row_count, step_count, model_width = hidden_states.shape
    top_count = routes.shape[2]
    hidden_part = w_down.shape[1]
    columns = model_width // replica_count
    tokens = row_count * step_count
    slot_count = min(tokens, max(MOST_BASE, 2 * tokens * top_count // expert_count))
    slot_count = -(-slot_count // replica_count) * replica_count
    part = slot_count // replica_count
    down_cols = exchange_gather(w_down[0], replica, replica_count)
    step_ids = lax.broadcasted_iota(jnp.int32, (row_count, step_count), 1)
    live_mask = ((step_ids < finish_step[:, None]) & (group_keep[0] == 1)).reshape(tokens)
    gate_share = route_weight / jnp.sum(route_weight, axis=2, keepdims=True)
    expert_ids = lax.broadcasted_iota(jnp.int32, (1, 1, expert_count), 2)
    picked = (routes.reshape(tokens, top_count, 1) == expert_ids) & live_mask[:, None, None]
    hit_mask = jnp.sum(picked.astype(jnp.int32), axis=1)
    share_wide = jnp.broadcast_to(gate_share.reshape(tokens, top_count, 1), picked.shape)
    weight = jnp.sum(jnp.where(picked, share_wide, jnp.zeros_like(share_wide)), axis=1)
    prior_hits = jnp.cumsum(hit_mask, axis=0) - hit_mask
    flat_inputs = hidden_states.reshape(tokens, model_width)
    chunks = 2 if part % 2 == 0 else 1
    sub = part // chunks
    member_ids = lax.broadcasted_iota(jnp.int32, (1, 1, replica_count, 1), 2)
    within_ids = lax.broadcasted_iota(jnp.int32, (1, 1, 1, sub), 3)
    combined = jnp.zeros((tokens, columns), jnp.float32)
    outgoings = []
    for chunk in range(chunks):
        slot_ids = replica * part + chunk * sub + lax.broadcasted_iota(jnp.int32, (1, 1, sub), 2)
        placement = (hit_mask[:, :, None] == 1) & (prior_hits[:, :, None] == slot_ids)
        placement = placement.reshape(tokens, expert_count * sub)
        outgoings.append(
            lax.dot_general(
                placement.astype(jnp.bfloat16),
                flat_inputs,
                (((0,), (0,)), ((), ())),
                preferred_element_type=jnp.float32,
            ).astype(jnp.bfloat16)
        )
    if chunks > 1:
        down_cols, outgoings[1] = lax.optimization_barrier((down_cols, outgoings[1]))
    down_stack = jnp.stack(down_cols, axis=0)
    for chunk in range(chunks):
        outgoing = outgoings[chunk]
        arrived = lax.all_to_all(outgoing, "expert", split_axis=0, concat_axis=0, tiled=True)
        gathered = lax.all_gather(arrived, "dp", axis=0, tiled=True)
        gate_part = jnp.dot(gathered, w_gate[0], preferred_element_type=jnp.float32)
        up_part = jnp.dot(gathered, w_up[0], preferred_element_type=jnp.float32)
        activated = (jax.nn.silu(gate_part) * up_part).astype(jnp.bfloat16)
        hidden_all = exchange_all(activated, replica_count)
        expert_cols = lax.dot_general(
            hidden_all, down_stack, (((0, 2), (0, 1)), ((), ())), preferred_element_type=jnp.float32
        ).astype(jnp.bfloat16)
        by_source = expert_cols.reshape(replica_count, expert_count, sub, columns).transpose(
            1, 0, 2, 3
        )
        returned_rows = lax.all_to_all(by_source, "expert", split_axis=0, concat_axis=0, tiled=True)
        all_slot_ids = member_ids * part + chunk * sub + within_ids
        weighted_place = jnp.where(
            (hit_mask[:, :, None, None] == 1) & (prior_hits[:, :, None, None] == all_slot_ids),
            weight[:, :, None, None],
            0.0,
        ).reshape(tokens, expert_count * replica_count * sub)
        combined = combined + jnp.dot(
            weighted_place,
            returned_rows.reshape(expert_count * replica_count * sub, columns).astype(jnp.float32),
            precision=lax.Precision.HIGH,
            preferred_element_type=jnp.float32,
        )
    share_rows = row_count // replica_count
    flat_device = dest_slot // share_rows
    target = flat_device // expert_count * share_rows + dest_slot % share_rows
    position_ids = lax.broadcasted_iota(jnp.int32, (replica_count * share_rows, row_count), 0)
    arrangement = (target[None, :] == position_ids).astype(jnp.bfloat16)
    arranged = jnp.dot(
        arrangement,
        combined.astype(jnp.bfloat16).reshape(row_count, step_count * columns),
        preferred_element_type=jnp.float32,
    ).astype(jnp.bfloat16)
    arranged = arranged.reshape(replica_count, share_rows, step_count, columns)
    quarters = lax.all_to_all(arranged, "dp", split_axis=0, concat_axis=0, tiled=True)
    return quarters.transpose(1, 2, 0, 3).reshape(share_rows, step_count, model_width)


def solution(mesh):
    in_specs = (
        P("expert", None, None),
        P("expert", None, None),
        P("expert", None, None),
        P("expert"),
        P("expert"),
        P("expert"),
        P("expert", None, "dp"),
        P("expert", None, "dp"),
        P("expert", "dp", None),
    )
    out_specs = P(("dp", "expert"), None, None)
    return jax.shard_map(body, mesh=mesh, in_specs=in_specs, out_specs=out_specs, check_vma=False)
```

profile of v0, /device:TPU:2, one launch (start us, length us, event | category | flops | bytes accessed | tf_op | source)
XLA Modules:
  0.0 302.3 jit_solution(9261390843322471953)
XLA Ops:
  6.5 3.7 %dynamic-slice_bitcast_fusion = (bf16[384,1024]{1,0:T(8,128)(2,1)}, bf16[384,1024]{1,0:T(8,128)(2,1)}, bf16[384,1024]{1,0:T(8,128)(2,1)}, bf16[384,1024]{1,0:T(8,128)(2,1)}) fusion(bf16[1,384,4096]{2,1,0:T(8,128)(2,1)} %param.17, s32[]{:T(128)S(6)} %select_n.63, s32[]{:T(128)S(6)} %select_n.59, s32[]{:T(128)S(6)} %select_n.57, s32[]{:T(128)S(6)} %select_n.61), kind=kLoop, calls=%fused_computation.40 | loop fusion | bytes 6291472 | tf_op jit(solution)/shard_map/dynamic_slice | solution.py:14
  10.3 1.6 collective-permute-start.3
  11.9 2.9 collective-permute-start.4
  14.8 1.3 collective-permute-start.5
  17.0 0.2 convert_reduce_fusion
  17.8 2.0 reshape.213
  19.7 2.4 convolution_convert_fusion
  22.2 9.0 %collective-permute-done.3 = bf16[384,1024]{1,0:T(8,128)(2,1)} collective-permute-done((bf16[384,1024]{1,0:T(8,128)(2,1)}, bf16[384,1024]{1,0:T(8,128)(2,1)}, u32[]{:S(2)}, u32[]{:S(2)}) %collective-permute-start.3) | collective-permute-done | bytes 786464 | tf_op jit(solution)/shard_map/ppermute | solution.py:16
  31.2 18.0 %collective-permute-done.4 = bf16[384,1024]{1,0:T(8,128)(2,1)} collective-permute-done((bf16[384,1024]{1,0:T(8,128)(2,1)}, bf16[384,1024]{1,0:T(8,128)(2,1)}, u32[]{:S(2)}, u32[]{:S(2)}) %collective-permute-start.4) | collective-permute-done | bytes 786464 | tf_op jit(solution)/shard_map/ppermute | solution.py:16
  49.2 2.5 all_to_all.29
  51.7 40.9 %all_to_all.39 = bf16[64,2,4096]{2,1,0:T(2,128)(2,1)} all-to-all(bf16[64,2,4096]{2,1,0:T(2,128)(2,1)} %all_to_all.29), channel_id=1, replica_groups=mesh['dp'=4,'expert'=64] {'expert'}, dimensions={0} | all-to-all | bytes 2097152 | tf_op jit(solution)/shard_map/all_to_all | solution.py:76
  92.7 2.3 all_to_all.31
  95.1 2.4 convolution_convert_fusion.1
  97.5 2.5 all_to_all.25
  100.1 34.6 %all_to_all.40 = bf16[64,2,4096]{2,1,0:T(2,128)(2,1)} all-to-all(bf16[64,2,4096]{2,1,0:T(2,128)(2,1)} %all_to_all.25), channel_id=1, replica_groups=mesh['dp'=4,'expert'=64] {'expert'}, dimensions={0} | all-to-all | bytes 2097152 | tf_op jit(solution)/shard_map/all_to_all | solution.py:76
  134.6 2.3 all_to_all.27
  136.9 5.0 %all-gather.5.cloned.1.call-done = bf16[512,4096]{1,0:T(8,128)(2,1)} async-done(((bf16[128,4096]{1,0:T(8,128)(2,1)}), bf16[512,4096]{1,0:T(8,128)(2,1)}) %all-gather.5.cloned.1.call-update) | async-done | bytes 4194320 | tf_op jit(solution)/shard_map/all_gather | solution.py:77
  142.0 4.7 %fusion.4 = f32[512,384]{1,0:T(8,128)S(1)} fusion(bf16[512,4096]{1,0:T(8,128)(2,1)} %all-gather.5.cloned.1.call-done, bf16[1,4096,384]{2,1,0:T(8,128)(2,1)S(1)} %copy-done), kind=kOutput, calls=%fused_computation.8 | convolution fusion | flops 1610612736 | bytes 8126464 | tf_op jit(solution)/shard_map/dot_general | solution.py:78
  146.7 2.3 fusion.28
  149.0 1.2 collective-permute-start.8
  150.2 1.8 collective-permute-start.7
  152.0 0.6 collective-permute-start.6
  152.6 9.2 %collective-permute-done.8 = bf16[512,384]{1,0:T(8,128)(2,1)S(1)} collective-permute-done((bf16[512,384]{1,0:T(8,128)(2,1)S(1)}, bf16[512,384]{1,0:T(8,128)(2,1)S(1)}, u32[]{:S(2)}, u32[]{:S(2)}) %collective-permute-start.8) | collective-permute-done | bytes 393248 | tf_op jit(solution)/shard_map/ppermute | solution.py:24
  161.8 4.5 %collective-permute-done.7 = bf16[512,384]{1,0:T(8,128)(2,1)S(1)} collective-permute-done((bf16[512,384]{1,0:T(8,128)(2,1)S(1)}, bf16[512,384]{1,0:T(8,128)(2,1)S(1)}, u32[]{:S(2)}, u32[]{:S(2)}) %collective-permute-start.7) | collective-permute-done | bytes 393248 | tf_op jit(solution)/shard_map/ppermute | solution.py:24
  166.3 14.4 %collective-permute-done.6 = bf16[512,384]{1,0:T(8,128)(2,1)S(1)} collective-permute-done((bf16[512,384]{1,0:T(8,128)(2,1)S(1)}, bf16[512,384]{1,0:T(8,128)(2,1)S(1)}, u32[]{:S(2)}, u32[]{:S(2)}) %collective-permute-start.6) | collective-permute-done | bytes 393248 | tf_op jit(solution)/shard_map/ppermute | solution.py:24
  180.7 4.5 %bitcast_convert_fusion = bf16[512,1024]{1,0:T(8,128)(2,1)} fusion(bf16[1,512,384]{2,1,0:T(8,128)(2,1)S(1)} %bitcast.91, bf16[1,512,384]{2,1,0:T(8,128)(2,1)S(1)} %bitcast.93, bf16[1,512,384]{2,1,0:T(8,128)(2,1)S(1)} %bitcast.94, bf16[1,512,384]{2,1,0:T(8,128)(2,1)S(1)} %bitcast.88, bf16[1,384,1024]{2,1,0:T(8,128)(2,1)} %bitcast.16, ...), kind=kOutput, calls=%fused_computation.12 | convolution fusion | flops 1618214912 | bytes 5767168 | tf_op jit(solution)/shard_map/dot_general | solution.py:82
  185.2 2.2 reshape.215
  187.5 3.4 %copy.47 = bf16[4,64,2,1024]{3,2,0,1:T(2,128)(2,1)} copy(bf16[4,64,2,1024]{3,2,1,0:T(2,128)(2,1)} %reshape.215) | data formatting | bytes 2097152 | tf_op jit(solution)/shard_map/reshape | solution.py:85
  190.8 10.7 %all-to-all-start.3 = ((bf16[64,4,2,1024]{3,2,1,0:T(2,128)(2,1)}), bf16[64,4,2,1024]{3,2,1,0:T(2,128)(2,1)}, u32[]{:S(2)}, u32[]{:S(2)}) async-start(bf16[64,4,2,1024]{3,2,1,0:T(2,128)(2,1)} %bitcast.79), calls=%async_computation.3 | async-start | bytes 2097152 | tf_op jit(solution)/shard_map/all_to_all | solution.py:88
  201.6 3.2 %all-gather.3.cloned.1.call-done = bf16[512,4096]{1,0:T(8,128)(2,1)} async-done(((bf16[128,4096]{1,0:T(8,128)(2,1)}), bf16[512,4096]{1,0:T(8,128)(2,1)}) %all-gather.3.cloned.1.call-update) | async-done | bytes 4194320 | tf_op jit(solution)/shard_map/all_gather | solution.py:77
  204.8 4.7 %fusion.6 = f32[512,384]{1,0:T(8,128)S(1)} fusion(bf16[512,4096]{1,0:T(8,128)(2,1)} %all-gather.3.cloned.1.call-done, bf16[1,4096,384]{2,1,0:T(8,128)(2,1)S(1)} %copy-done), kind=kOutput, calls=%fused_computation.10 | convolution fusion | flops 1610612736 | bytes 8126464 | tf_op jit(solution)/shard_map/dot_general | solution.py:78
  209.5 2.3 fusion.31
  211.8 0.7 collective-permute-start.2
  212.5 1.8 collective-permute-start.1
  214.3 0.8 collective-permute-start
  215.1 8.8 %collective-permute-done.2 = bf16[512,384]{1,0:T(8,128)(2,1)S(1)} collective-permute-done((bf16[512,384]{1,0:T(8,128)(2,1)S(1)}, bf16[512,384]{1,0:T(8,128)(2,1)S(1)}, u32[]{:S(2)}, u32[]{:S(2)}) %collective-permute-start.2) | collective-permute-done | bytes 393248 | tf_op jit(solution)/shard_map/ppermute | solution.py:24
  223.9 2.2 collective-permute-done.1
  226.1 7.2 %collective-permute-done = bf16[512,384]{1,0:T(8,128)(2,1)S(1)} collective-permute-done((bf16[512,384]{1,0:T(8,128)(2,1)S(1)}, bf16[512,384]{1,0:T(8,128)(2,1)S(1)}, u32[]{:S(2)}, u32[]{:S(2)}) %collective-permute-start) | collective-permute-done | bytes 393248 | tf_op jit(solution)/shard_map/ppermute | solution.py:24
  233.3 4.4 %bitcast_convert_fusion.1 = bf16[512,1024]{1,0:T(8,128)(2,1)} fusion(bf16[1,512,384]{2,1,0:T(8,128)(2,1)S(1)} %bitcast.89, bf16[1,512,384]{2,1,0:T(8,128)(2,1)S(1)} %bitcast.90, bf16[1,512,384]{2,1,0:T(8,128)(2,1)S(1)} %bitcast.92, bf16[1,512,384]{2,1,0:T(8,128)(2,1)S(1)} %bitcast.87, bf16[1,384,1024]{2,1,0:T(8,128)(2,1)} %bitcast.16, ...), kind=kOutput, calls=%fused_computation.13 | convolution fusion | flops 1618214912 | bytes 5767168 | tf_op jit(solution)/shard_map/dot_general | solution.py:82
  237.7 2.3 reshape.214
  239.9 3.4 %copy.48 = bf16[4,64,2,1024]{3,2,0,1:T(2,128)(2,1)} copy(bf16[4,64,2,1024]{3,2,1,0:T(2,128)(2,1)} %reshape.214) | data formatting | bytes 2097152 | tf_op jit(solution)/shard_map/reshape | solution.py:85
  243.3 10.7 %all-to-all-start.1 = ((bf16[64,4,2,1024]{3,2,1,0:T(2,128)(2,1)}), bf16[64,4,2,1024]{3,2,1,0:T(2,128)(2,1)}, u32[]{:S(2)}, u32[]{:S(2)}) async-start(bf16[64,4,2,1024]{3,2,1,0:T(2,128)(2,1)} %bitcast.80), calls=%async_computation.1 | async-start | bytes 2097152 | tf_op jit(solution)/shard_map/all_to_all | solution.py:88
  254.2 0.3 select_reduce_fusion
  254.7 3.5 %convolution_bitcast_fusion = f32[64,1024]{1,0:T(8,128)} fusion(bf16[64,4,2,1024]{3,2,1,0:T(2,128)(2,1)} %all-to-all-done.3, s32[4,2]{1,0:T(4,128)S(1)} %iota_add_fusion, f32[64,64]{1,0:T(8,128)S(1)} %select_reduce_fusion, s32[64,64]{1,0:T(8,128)S(1)} %sub.20, pred[64,64]{1,0:T(8,128)(4,1)S(1)} %broadcast_compare_fusion), kind=kOutput, calls=%fused_computation.32 | convolution fusion | flops 201424896 | bytes 1347616 | tf_op jit(solution)/shard_map/dot_general | solution.py:95
  258.2 24.6 %all-to-all-done.1 = bf16[64,4,2,1024]{3,2,1,0:T(2,128)(2,1)} async-done(((bf16[64,4,2,1024]{3,2,1,0:T(2,128)(2,1)}), bf16[64,4,2,1024]{3,2,1,0:T(2,128)(2,1)}, u32[]{:S(2)}, u32[]{:S(2)}) %all-to-all-start.1) | async-done | bytes 1048608 | tf_op jit(solution)/shard_map/all_to_all | solution.py:88
  282.8 2.8 fusion.35
  285.9 8.8 %all_to_all.41 = bf16[4,4,4,1024]{3,2,1,0:T(4,128)(2,1)S(1)} all-to-all(bf16[4,4,4,1024]{3,2,1,0:T(4,128)(2,1)S(1)} %reshape.217), channel_id=1, replica_groups=mesh['dp'=4,'expert'=64] {'dp'}, dimensions={0} | all-to-all | bytes 262144 | tf_op jit(solution)/shard_map/all_to_all | solution.py:112
  294.7 0.7 copy.40
  (51 shorter events, 1.5 us)
Async XLA Ops:
  6.5 135.4 %copy-start = (bf16[1,4096,384]{2,1,0:T(8,128)(2,1)S(1)}, bf16[1,4096,384]{2,1,0:T(8,128)(2,1)}, u32[]{:S(2)}) copy-start(bf16[1,4096,384]{2,1,0:T(8,128)(2,1)} %param.15) | copy-start | bytes 9437188
  6.5 135.4 %all-gather.5.cloned.1.call-start = ((), (), s32[]{:S(2)}) async-start(), calls=%async_computation.6 | async-start | bytes 5242880 | tf_op jit(solution)/shard_map/all_gather | solution.py:77
  6.5 9.6 %copy-start.4 = (s32[16,4,8]{0,2,1:T(8,128)S(1)}, s32[16,4,8]{0,2,1:T(8,128)}, u32[]{:S(2)}) copy-start(s32[16,4,8]{0,2,1:T(8,128)} %param.10) | copy-start | bytes 6148
  6.5 10.3 %copy-start.5 = (s32[16]{0:T(128)S(1)}, s32[16]{0:T(128)}, u32[]{:S(2)}) copy-start(s32[16]{0:T(128)} %param.12) | copy-start | bytes 196
  10.3 20.9 %collective-permute-start.3 = (bf16[384,1024]{1,0:T(8,128)(2,1)}, bf16[384,1024]{1,0:T(8,128)(2,1)}, u32[]{:S(2)}, u32[]{:S(2)}) collective-permute-start(bf16[384,1024]{1,0:T(8,128)(2,1)} %get-tuple-element.16), channel_id=1, source_target_pairs={{0,64},{64,128},{128,192},{192,0},{1,65},{65,129},{129,193},{193,1... | collective-permute-start | bytes 2359304 | tf_op jit(solution)/shard_map/ppermute | solution.py:16
  11.9 37.3 %collective-permute-start.4 = (bf16[384,1024]{1,0:T(8,128)(2,1)}, bf16[384,1024]{1,0:T(8,128)(2,1)}, u32[]{:S(2)}, u32[]{:S(2)}) collective-permute-start(bf16[384,1024]{1,0:T(8,128)(2,1)} %get-tuple-element.18), channel_id=1, source_target_pairs={{0,128},{64,192},{128,0},{192,64},{1,129},{65,193},{129,1},{193,65... | collective-permute-start | bytes 2359304 | tf_op jit(solution)/shard_map/ppermute | solution.py:16
  14.8 34.4 %collective-permute-start.5 = (bf16[384,1024]{1,0:T(8,128)(2,1)}, bf16[384,1024]{1,0:T(8,128)(2,1)}, u32[]{:S(2)}, u32[]{:S(2)}) collective-permute-start(bf16[384,1024]{1,0:T(8,128)(2,1)} %get-tuple-element.15), channel_id=1, source_target_pairs={{0,192},{64,0},{128,64},{192,128},{1,193},{65,1},{129,65},{193,129... | collective-permute-start | bytes 2359304 | tf_op jit(solution)/shard_map/ppermute | solution.py:16
  95.0 109.8 %all-gather.3.cloned.1.call-start = ((), (), s32[]{:S(2)}) async-start(), calls=%async_computation.5 | async-start | bytes 5242880 | tf_op jit(solution)/shard_map/all_gather | solution.py:77
  142.0 4.7 %copy-start.7 = (bf16[512,4096]{1,0:T(8,128)(2,1)S(1)}, bf16[512,4096]{1,0:T(8,128)(2,1)}, u32[]{:S(2)}) copy-start(bf16[512,4096]{1,0:T(8,128)(2,1)} %all-gather.5.cloned.1.call-done) | copy-start | bytes 12582916
  142.0 4.7 %copy-start.8 = (bf16[1,4096,384]{2,1,0:T(8,128)(2,1)S(1)}, bf16[1,4096,384]{2,1,0:T(8,128)(2,1)}, u32[]{:S(2)}) copy-start(bf16[1,4096,384]{2,1,0:T(8,128)(2,1)} %param.16) | copy-start | bytes 9437188
  146.6 34.1 %copy-start.1 = (bf16[384,1024]{1,0:T(8,128)(2,1)S(1)}, bf16[384,1024]{1,0:T(8,128)(2,1)}, u32[]{:S(2)}) copy-start(bf16[384,1024]{1,0:T(8,128)(2,1)} %get-tuple-element.10) | copy-start | bytes 2359300
  149.0 12.8 %collective-permute-start.8 = (bf16[512,384]{1,0:T(8,128)(2,1)S(1)}, bf16[512,384]{1,0:T(8,128)(2,1)S(1)}, u32[]{:S(2)}, u32[]{:S(2)}) collective-permute-start(bf16[512,384]{1,0:T(8,128)(2,1)S(1)} %fusion.28), channel_id=1, source_target_pairs={{0,192},{64,0},{128,64},{192,128},{1,193},{65,1},{129,65},{193,129... | collective-permute-start | bytes 1179656 | tf_op jit(solution)/shard_map/ppermute | solution.py:24
  150.2 16.1 %collective-permute-start.7 = (bf16[512,384]{1,0:T(8,128)(2,1)S(1)}, bf16[512,384]{1,0:T(8,128)(2,1)S(1)}, u32[]{:S(2)}, u32[]{:S(2)}) collective-permute-start(bf16[512,384]{1,0:T(8,128)(2,1)S(1)} %fusion.28), channel_id=1, source_target_pairs={{0,128},{64,192},{128,0},{192,64},{1,129},{65,193},{129,1},{193,65... | collective-permute-start | bytes 1179656 | tf_op jit(solution)/shard_map/ppermute | solution.py:24
  152.0 28.7 %collective-permute-start.6 = (bf16[512,384]{1,0:T(8,128)(2,1)S(1)}, bf16[512,384]{1,0:T(8,128)(2,1)S(1)}, u32[]{:S(2)}, u32[]{:S(2)}) collective-permute-start(bf16[512,384]{1,0:T(8,128)(2,1)S(1)} %fusion.28), channel_id=1, source_target_pairs={{0,64},{64,128},{128,192},{192,0},{1,65},{65,129},{129,193},{193,1... | collective-permute-start | bytes 1179656 | tf_op jit(solution)/shard_map/ppermute | solution.py:24
  190.8 52.5 %all-to-all-start.3 = ((bf16[64,4,2,1024]{3,2,1,0:T(2,128)(2,1)}), bf16[64,4,2,1024]{3,2,1,0:T(2,128)(2,1)}, u32[]{:S(2)}, u32[]{:S(2)}) async-start(bf16[64,4,2,1024]{3,2,1,0:T(2,128)(2,1)} %bitcast.79), calls=%async_computation.3 | async-start | bytes 2097152 | tf_op jit(solution)/shard_map/all_to_all | solution.py:88
  204.8 4.7 %copy-start.6 = (bf16[512,4096]{1,0:T(8,128)(2,1)S(1)}, bf16[512,4096]{1,0:T(8,128)(2,1)}, u32[]{:S(2)}) copy-start(bf16[512,4096]{1,0:T(8,128)(2,1)} %all-gather.3.cloned.1.call-done) | copy-start | bytes 12582916
  204.8 4.7 %copy-start.9 = (bf16[1,4096,384]{2,1,0:T(8,128)(2,1)S(1)}, bf16[1,4096,384]{2,1,0:T(8,128)(2,1)}, u32[]{:S(2)}) copy-start(bf16[1,4096,384]{2,1,0:T(8,128)(2,1)} %param.16) | copy-start | bytes 9437188
  209.5 23.8 %copy-start.2 = (bf16[384,1024]{1,0:T(8,128)(2,1)S(1)}, bf16[384,1024]{1,0:T(8,128)(2,1)}, u32[]{:S(2)}) copy-start(bf16[384,1024]{1,0:T(8,128)(2,1)} %get-tuple-element.10) | copy-start | bytes 2359300
  211.8 12.0 %collective-permute-start.2 = (bf16[512,384]{1,0:T(8,128)(2,1)S(1)}, bf16[512,384]{1,0:T(8,128)(2,1)S(1)}, u32[]{:S(2)}, u32[]{:S(2)}) collective-permute-start(bf16[512,384]{1,0:T(8,128)(2,1)S(1)} %fusion.31), channel_id=1, source_target_pairs={{0,192},{64,0},{128,64},{192,128},{1,193},{65,1},{129,65},{193,129... | collective-permute-start | bytes 1179656 | tf_op jit(solution)/shard_map/ppermute | solution.py:24
  212.5 13.6 %collective-permute-start.1 = (bf16[512,384]{1,0:T(8,128)(2,1)S(1)}, bf16[512,384]{1,0:T(8,128)(2,1)S(1)}, u32[]{:S(2)}, u32[]{:S(2)}) collective-permute-start(bf16[512,384]{1,0:T(8,128)(2,1)S(1)} %fusion.31), channel_id=1, source_target_pairs={{0,128},{64,192},{128,0},{192,64},{1,129},{65,193},{129,1},{193,65... | collective-permute-start | bytes 1179656 | tf_op jit(solution)/shard_map/ppermute | solution.py:24
  214.3 18.9 %collective-permute-start = (bf16[512,384]{1,0:T(8,128)(2,1)S(1)}, bf16[512,384]{1,0:T(8,128)(2,1)S(1)}, u32[]{:S(2)}, u32[]{:S(2)}) collective-permute-start(bf16[512,384]{1,0:T(8,128)(2,1)S(1)} %fusion.31), channel_id=1, source_target_pairs={{0,64},{64,128},{128,192},{192,0},{1,65},{65,129},{129,193},{193,1... | collective-permute-start | bytes 1179656 | tf_op jit(solution)/shard_map/ppermute | solution.py:24
  237.7 16.4 %copy-start.3 = (f32[16,4,8]{0,2,1:T(8,128)S(1)}, f32[16,4,8]{0,2,1:T(8,128)}, u32[]{:S(2)}) copy-start(f32[16,4,8]{0,2,1:T(8,128)} %param.11) | copy-start | bytes 6148
  237.7 16.8 %copy-start.10 = (s32[16]{0:T(128)S(1)}, s32[16]{0:T(128)}, u32[]{:S(2)}) copy-start(s32[16]{0:T(128)} %param.14) | copy-start | bytes 196
  243.3 39.5 %all-to-all-start.1 = ((bf16[64,4,2,1024]{3,2,1,0:T(2,128)(2,1)}), bf16[64,4,2,1024]{3,2,1,0:T(2,128)(2,1)}, u32[]{:S(2)}, u32[]{:S(2)}) async-start(bf16[64,4,2,1024]{3,2,1,0:T(2,128)(2,1)} %bitcast.80), calls=%async_computation.1 | async-start | bytes 2097152 | tf_op jit(solution)/shard_map/all_to_all | solution.py:88
Sparse Core Ops, SparseCore 0:
  95.1 46.8 all-gather.4
  143.8 60.9 all-gather.2
where the time goes:
time: 303 us; the launch traced here: 302 us
  waiting for transfers between devices  106 us (35%)
  blocking collectives  84.3 us (28%)
  matrix products  34.3 us (11%)
  starting transfers between devices  34.2 us (11%)
  local copies, waits for them, and re-layouts  28 us (9%)
  between operations  14.3 us (5%)
    all_to_all x2, blocking collectives, body(): lax.all_to_all(outgoing, 'expert', split_axis=0, concat_axis=0, tiled=True)  75.5 us
    ppermute x6, waiting for transfers between devices, exchange_all(): pieces.append(lax.ppermute(block, 'dp', pairs))  46.3 us
    ppermute x3, waiting for transfers between devices, exchange_gather(): pieces.append(lax.ppermute(outgoing, 'dp', pairs))  27 us
    all_to_all x2, waiting for transfers between devices, body(): lax.all_to_all(by_source, 'expert', split_axis=0, concat_axis=0, tiled=True)  24.6 us
    all_to_all x2, starting transfers between devices, body(): lax.all_to_all(by_source, 'expert', split_axis=0, concat_axis=0, tiled=True)  21.5 us
    reshape x4, local copies, waits for them, and re-layouts, body(): expert_cols.reshape(replica_count, expert_count, sub, columns)  11.2 us
    all_to_all x4, local copies, waits for them, and re-layouts, body(): lax.all_to_all(outgoing, 'expert', split_axis=0, concat_axis=0, tiled=True)  9.66 us
    dot_general x2, matrix products, body(): gate_part = jnp.dot(gathered, w_gate[0], preferred_element_type=jnp.float32)  9.32 us
  transfers between devices with their start and end apart: 13, of which 11 were waited for; matrix products, arithmetic and copies ran while one was open for 15% of the time, Pallas kernels for 0%

commit v1 on v0

--- a/solution.py
+++ b/solution.py
@@ -74,7 +74,11 @@
     for chunk in range(chunks):
         outgoing = outgoings[chunk]
         arrived = lax.all_to_all(outgoing, "expert", split_axis=0, concat_axis=0, tiled=True)
-        gathered = lax.all_gather(arrived, "dp", axis=0, tiled=True)
+        state_marks = lambda slab_in: jnp.concatenate(
+            lax.all_to_all(jnp.stack([slab_in for _ in range(lax.axis_size("dp"))]), "dp", 0, 0),
+            axis=0,
+        )
+        gathered = state_marks(arrived)
         gate_part = jnp.dot(gathered, w_gate[0], preferred_element_type=jnp.float32)
         up_part = jnp.dot(gathered, w_up[0], preferred_element_type=jnp.float32)
         activated = (jax.nn.silu(gate_part) * up_part).astype(jnp.bfloat16)

time: 303 us -> 363 us (1.20)
  waiting for transfers between devices: 106 us -> 216 us
  blocking collectives: 84.3 us -> 8.51 us
  starting transfers between devices: 34.2 us -> 60.2 us
  between operations: 14.3 us -> 0.93 us
  local copies, waits for them, and re-layouts: 28 us -> 35.5 us
  matrix products: 34.3 us -> 38.9 us
    all_to_all x0 -> x4, waiting for transfers between devices: none -> 96 us  [the longest x2 50.1 us: body(): lax.all_to_all(outgoing, 'expert', split_axis=0, concat_axis=0, tiled=True)]
    all_to_all x2 -> x0, blocking collectives: 75.5 us -> none  [body(): lax.all_to_all(outgoing, 'expert', split_axis=0, concat_axis=0, tiled=True)]
    all_to_all x0 -> x4, starting transfers between devices: none -> 27.8 us  [the longest x2 18 us: body(): lax.all_to_all(outgoing, 'expert', split_axis=0, concat_axis=0, tiled=True)]
    ppermute x6, waiting for transfers between devices: 46.3 us -> 68.7 us  [exchange_all(): pieces.append(lax.ppermute(block, 'dp', pairs))]
    another operation x0 -> x4, local copies, waits for them, and re-layouts: none -> 11.9 us  [body(): jnp.stack([slab_in for _ in range(lax.axis_size('dp'))])]
    all_gather x2 -> x0, waiting for transfers between devices: 8.25 us -> none  [body(): gathered = lax.all_gather(arrived, 'dp', axis=0, tiled=True)]
    all_to_all x4 -> x2, local copies, waits for them, and re-layouts: 9.66 us -> 5.07 us  [body(): lax.all_to_all(outgoing, 'expert', split_axis=0, concat_axis=0, tiled=True)]
    dot_general x2, matrix products: 4.69 us -> 9.26 us  [body(): up_part = jnp.dot(gathered, w_up[0], preferred_element_type=jnp.float32)]
  transfers between devices with their start and end apart: 13 -> 15, of which waited for: 11 -> 12; matrix products, arithmetic and copies ran while one was open for 15% -> 15% of each run, Pallas kernels for 0% -> 0%
where the time goes in v1:
time: 363 us; the launch traced here: 361 us
  waiting for transfers between devices  216 us (60%)
  starting transfers between devices  60.2 us (17%)
  matrix products  38.9 us (11%)
  local copies, waits for them, and re-layouts  35.5 us (10%)
  blocking collectives  8.51 us (2%)
    ppermute x6, waiting for transfers between devices, exchange_all(): pieces.append(lax.ppermute(block, 'dp', pairs))  68.7 us
    all_to_all x2, waiting for transfers between devices, body(): lax.all_to_all(outgoing, 'expert', split_axis=0, concat_axis=0, tiled=True)  50.1 us
    all_to_all x2, waiting for transfers between devices, body(): lax.all_to_all(jnp.stack([slab_in for _ in range(lax.axis_size('dp'))]),...  45.9 us
    ppermute x3, waiting for transfers between devices, exchange_gather(): pieces.append(lax.ppermute(outgoing, 'dp', pairs))  27 us
    all_to_all x2, waiting for transfers between devices, body(): lax.all_to_all(by_source, 'expert', split_axis=0, concat_axis=0, tiled=True)  24.6 us
    all_to_all x2, starting transfers between devices, body(): lax.all_to_all(by_source, 'expert', split_axis=0, concat_axis=0, tiled=True)  18.5 us
    all_to_all x2, starting transfers between devices, body(): lax.all_to_all(outgoing, 'expert', split_axis=0, concat_axis=0, tiled=True)  18 us
    another operation x4, local copies, waits for them, and re-layouts, body(): jnp.stack([slab_in for _ in range(lax.axis_size('dp'))])  11.9 us
  transfers between devices with their start and end apart: 15, of which 12 were waited for; matrix products, arithmetic and copies ran while one was open for 15% of the time, Pallas kernels for 0%

profile of v1, /device:TPU:2, one launch (start us, length us, event | category | flops | bytes accessed | tf_op | source)
XLA Modules:
  0.0 361.5 jit_solution(16574425634818592104)
XLA Ops:
  0.0 3.7 %dynamic-slice_bitcast_fusion = (bf16[384,1024]{1,0:T(8,128)(2,1)}, bf16[384,1024]{1,0:T(8,128)(2,1)}, bf16[384,1024]{1,0:T(8,128)(2,1)}, bf16[384,1024]{1,0:T(8,128)(2,1)}) fusion(bf16[1,384,4096]{2,1,0:T(8,128)(2,1)} %param.17, s32[]{:T(128)S(6)} %select_n.63, s32[]{:T(128)S(6)} %select_n.59, s32[]{:T(128)S(6)} %select_n.57, s32[]{:T(128)S(6)} %select_n.61), kind=kLoop, calls=%fused_computation.40 | loop fusion | bytes 6291472 | tf_op jit(solution)/shard_map/dynamic_slice | solution.py:14
  3.7 1.6 collective-permute-start.3
  5.3 2.9 collective-permute-start.4
  8.2 1.3 collective-permute-start.5
  11.2 2.0 reshape.225
  13.2 2.4 convolution_convert_fusion
  15.6 9.0 %collective-permute-done.3 = bf16[384,1024]{1,0:T(8,128)(2,1)} collective-permute-done((bf16[384,1024]{1,0:T(8,128)(2,1)}, bf16[384,1024]{1,0:T(8,128)(2,1)}, u32[]{:S(2)}, u32[]{:S(2)}) %collective-permute-start.3) | collective-permute-done | bytes 786464 | tf_op jit(solution)/shard_map/ppermute | solution.py:16
  24.6 18.0 %collective-permute-done.4 = bf16[384,1024]{1,0:T(8,128)(2,1)} collective-permute-done((bf16[384,1024]{1,0:T(8,128)(2,1)}, bf16[384,1024]{1,0:T(8,128)(2,1)}, u32[]{:S(2)}, u32[]{:S(2)}) %collective-permute-start.4) | collective-permute-done | bytes 786464 | tf_op jit(solution)/shard_map/ppermute | solution.py:16
  42.6 2.5 all_to_all.31
  45.2 12.2 %all-to-all-start.3 = ((bf16[64,2,4096]{2,1,0:T(2,128)(2,1)}), bf16[64,2,4096]{2,1,0:T(2,128)(2,1)}, u32[]{:S(2)}, u32[]{:S(2)}) async-start(bf16[64,2,4096]{2,1,0:T(2,128)(2,1)} %all_to_all.31), calls=%async_computation.3 | async-start | bytes 2097152 | tf_op jit(solution)/shard_map/all_to_all | solution.py:76
  57.4 2.4 convolution_convert_fusion.1
  59.9 2.5 all_to_all.27
  62.4 23.7 %all-to-all-done.3 = bf16[64,2,4096]{2,1,0:T(2,128)(2,1)} async-done(((bf16[64,2,4096]{2,1,0:T(2,128)(2,1)}), bf16[64,2,4096]{2,1,0:T(2,128)(2,1)}, u32[]{:S(2)}, u32[]{:S(2)}) %all-to-all-start.3) | async-done | bytes 1048608 | tf_op jit(solution)/shard_map/all_to_all | solution.py:76
  86.1 5.8 %all-to-all-start = ((bf16[64,2,4096]{2,1,0:T(2,128)(2,1)}), bf16[64,2,4096]{2,1,0:T(2,128)(2,1)}, u32[]{:S(2)}, u32[]{:S(2)}) async-start(bf16[64,2,4096]{2,1,0:T(2,128)(2,1)} %all_to_all.27), calls=%async_computation | async-start | bytes 2097152 | tf_op jit(solution)/shard_map/all_to_all | solution.py:76
  92.0 2.3 stack.75
  94.2 26.4 %all-to-all-done = bf16[64,2,4096]{2,1,0:T(2,128)(2,1)} async-done(((bf16[64,2,4096]{2,1,0:T(2,128)(2,1)}), bf16[64,2,4096]{2,1,0:T(2,128)(2,1)}, u32[]{:S(2)}, u32[]{:S(2)}) %all-to-all-start) | async-done | bytes 1048608 | tf_op jit(solution)/shard_map/all_to_all | solution.py:76
  120.7 3.7 %stack.76 = bf16[4,128,4096]{2,1,0:T(8,128)(2,1)} broadcast(bf16[128,4096]{1,0:T(8,128)(2,1)} %stack.75), dimensions={1,2} | broadcast | bytes 5242880 | tf_op jit(solution)/shard_map/stack | solution.py:78
  124.3 4.9 %all-to-all-start.4 = ((bf16[4,128,4096]{2,1,0:T(8,128)(2,1)}), bf16[4,128,4096]{2,1,0:T(8,128)(2,1)}, u32[]{:S(2)}, u32[]{:S(2)}) async-start(bf16[4,128,4096]{2,1,0:T(8,128)(2,1)} %stack.76), calls=%async_computation.4 | async-start | bytes 8388608 | tf_op jit(solution)/shard_map/all_to_all | solution.py:78
  129.3 2.3 stack.63
  131.6 45.9 %all-to-all-done.4 = bf16[4,128,4096]{2,1,0:T(8,128)(2,1)} async-done(((bf16[4,128,4096]{2,1,0:T(8,128)(2,1)}), bf16[4,128,4096]{2,1,0:T(8,128)(2,1)}, u32[]{:S(2)}, u32[]{:S(2)}) %all-to-all-start.4) | async-done | bytes 4194336 | tf_op jit(solution)/shard_map/all_to_all | solution.py:78
  177.4 3.7 %stack.64 = bf16[4,128,4096]{2,1,0:T(8,128)(2,1)} broadcast(bf16[128,4096]{1,0:T(8,128)(2,1)} %stack.63), dimensions={1,2} | broadcast | bytes 5242880 | tf_op jit(solution)/shard_map/stack | solution.py:78
  181.2 4.9 %all-to-all-start.1 = ((bf16[4,128,4096]{2,1,0:T(8,128)(2,1)}), bf16[4,128,4096]{2,1,0:T(8,128)(2,1)}, u32[]{:S(2)}, u32[]{:S(2)}) async-start(bf16[4,128,4096]{2,1,0:T(8,128)(2,1)} %stack.64), calls=%async_computation.1 | async-start | bytes 8388608 | tf_op jit(solution)/shard_map/all_to_all | solution.py:78
  186.0 4.7 %fusion.4 = f32[512,384]{1,0:T(8,128)S(1)} fusion(bf16[512,4096]{1,0:T(8,128)(2,1)} %bitcast.22, bf16[1,4096,384]{2,1,0:T(8,128)(2,1)S(1)} %copy-done), kind=kOutput, calls=%fused_computation.8 | convolution fusion | flops 1610612736 | bytes 8126464 | tf_op jit(solution)/shard_map/dot_general | solution.py:82
  190.7 4.6 %fusion.28 = bf16[512,384]{1,0:T(8,128)(2,1)S(1)} fusion(bf16[512,4096]{1,0:T(8,128)(2,1)} %bitcast.22, bf16[1,4096,384]{2,1,0:T(8,128)(2,1)S(1)} %copy-done.6, f32[512,384]{1,0:T(8,128)S(1)} %fusion.4), kind=kOutput, calls=%fused_computation.30 | convolution fusion | flops 1611792384 | bytes 8519680 | tf_op jit(solution)/shard_map/dot_general | solution.py:83
  195.4 3.3 collective-permute-start.8
  199.5 0.9 collective-permute-start.6
  200.3 42.9 %collective-permute-done.8 = bf16[512,384]{1,0:T(8,128)(2,1)S(1)} collective-permute-done((bf16[512,384]{1,0:T(8,128)(2,1)S(1)}, bf16[512,384]{1,0:T(8,128)(2,1)S(1)}, u32[]{:S(2)}, u32[]{:S(2)}) %collective-permute-start.8) | collective-permute-done | bytes 393248 | tf_op jit(solution)/shard_map/ppermute | solution.py:24
  243.2 1.5 collective-permute-done.7
  244.7 5.0 %collective-permute-done.6 = bf16[512,384]{1,0:T(8,128)(2,1)S(1)} collective-permute-done((bf16[512,384]{1,0:T(8,128)(2,1)S(1)}, bf16[512,384]{1,0:T(8,128)(2,1)S(1)}, u32[]{:S(2)}, u32[]{:S(2)}) %collective-permute-start.6) | collective-permute-done | bytes 393248 | tf_op jit(solution)/shard_map/ppermute | solution.py:24
  249.7 4.5 %bitcast_convert_fusion = bf16[512,1024]{1,0:T(8,128)(2,1)} fusion(bf16[1,512,384]{2,1,0:T(8,128)(2,1)S(1)} %bitcast.93, bf16[1,512,384]{2,1,0:T(8,128)(2,1)S(1)} %bitcast.95, bf16[1,512,384]{2,1,0:T(8,128)(2,1)S(1)} %bitcast.96, bf16[1,512,384]{2,1,0:T(8,128)(2,1)S(1)} %bitcast.90, bf16[1,384,1024]{2,1,0:T(8,128)(2,1)} %bitcast.17, ...), kind=kOutput, calls=%fused_computation.12 | convolution fusion | flops 1618214912 | bytes 5767168 | tf_op jit(solution)/shard_map/dot_general | solution.py:86
  254.2 2.3 reshape.229
  256.5 3.5 copy.47
  260.0 8.1 %all-to-all-start.5 = ((bf16[64,4,2,1024]{3,2,1,0:T(2,128)(2,1)}), bf16[64,4,2,1024]{3,2,1,0:T(2,128)(2,1)}, u32[]{:S(2)}, u32[]{:S(2)}) async-start(bf16[64,4,2,1024]{3,2,1,0:T(2,128)(2,1)} %bitcast.81), calls=%async_computation.5 | async-start | bytes 2097152 | tf_op jit(solution)/shard_map/all_to_all | solution.py:92
  268.0 4.7 %fusion.6 = f32[512,384]{1,0:T(8,128)S(1)} fusion(bf16[512,4096]{1,0:T(8,128)(2,1)} %bitcast.3, bf16[1,4096,384]{2,1,0:T(8,128)(2,1)S(1)} %copy-done), kind=kOutput, calls=%fused_computation.10 | convolution fusion | flops 1610612736 | bytes 8126464 | tf_op jit(solution)/shard_map/dot_general | solution.py:82
  272.7 4.6 %fusion.31 = bf16[512,384]{1,0:T(8,128)(2,1)S(1)} fusion(bf16[512,4096]{1,0:T(8,128)(2,1)} %bitcast.3, bf16[1,4096,384]{2,1,0:T(8,128)(2,1)S(1)} %copy-done.7, f32[512,384]{1,0:T(8,128)S(1)} %fusion.6), kind=kOutput, calls=%fused_computation.31 | convolution fusion | flops 1611792384 | bytes 8519680 | tf_op jit(solution)/shard_map/dot_general | solution.py:83
  277.4 1.6 collective-permute-start.2
  279.0 1.5 collective-permute-start.1
  280.4 9.0 %collective-permute-done.2 = bf16[512,384]{1,0:T(8,128)(2,1)S(1)} collective-permute-done((bf16[512,384]{1,0:T(8,128)(2,1)S(1)}, bf16[512,384]{1,0:T(8,128)(2,1)S(1)}, u32[]{:S(2)}, u32[]{:S(2)}) %collective-permute-start.2) | collective-permute-done | bytes 393248 | tf_op jit(solution)/shard_map/ppermute | solution.py:24
  289.4 3.1 collective-permute-done.1
  292.5 7.3 %collective-permute-done = bf16[512,384]{1,0:T(8,128)(2,1)S(1)} collective-permute-done((bf16[512,384]{1,0:T(8,128)(2,1)S(1)}, bf16[512,384]{1,0:T(8,128)(2,1)S(1)}, u32[]{:S(2)}, u32[]{:S(2)}) %collective-permute-start) | collective-permute-done | bytes 393248 | tf_op jit(solution)/shard_map/ppermute | solution.py:24
  299.8 4.4 %bitcast_convert_fusion.1 = bf16[512,1024]{1,0:T(8,128)(2,1)} fusion(bf16[1,512,384]{2,1,0:T(8,128)(2,1)S(1)} %bitcast.91, bf16[1,512,384]{2,1,0:T(8,128)(2,1)S(1)} %bitcast.92, bf16[1,512,384]{2,1,0:T(8,128)(2,1)S(1)} %bitcast.94, bf16[1,512,384]{2,1,0:T(8,128)(2,1)S(1)} %bitcast.89, bf16[1,384,1024]{2,1,0:T(8,128)(2,1)} %bitcast.17, ...), kind=kOutput, calls=%fused_computation.13 | convolution fusion | flops 1618214912 | bytes 5767168 | tf_op jit(solution)/shard_map/dot_general | solution.py:86
  304.2 2.3 reshape.227
  306.5 3.4 copy.48
  309.9 10.5 %all-to-all-start.2 = ((bf16[64,4,2,1024]{3,2,1,0:T(2,128)(2,1)}), bf16[64,4,2,1024]{3,2,1,0:T(2,128)(2,1)}, u32[]{:S(2)}, u32[]{:S(2)}) async-start(bf16[64,4,2,1024]{3,2,1,0:T(2,128)(2,1)} %bitcast.82), calls=%async_computation.2 | async-start | bytes 2097152 | tf_op jit(solution)/shard_map/all_to_all | solution.py:92
  321.0 3.5 convolution_bitcast_fusion
  324.5 24.6 %all-to-all-done.2 = bf16[64,4,2,1024]{3,2,1,0:T(2,128)(2,1)} async-done(((bf16[64,4,2,1024]{3,2,1,0:T(2,128)(2,1)}), bf16[64,4,2,1024]{3,2,1,0:T(2,128)(2,1)}, u32[]{:S(2)}, u32[]{:S(2)}) %all-to-all-start.2) | async-done | bytes 1048608 | tf_op jit(solution)/shard_map/all_to_all | solution.py:92
  349.1 2.8 fusion.35
  352.3 8.5 %all_to_all.43 = bf16[4,4,4,1024]{3,2,1,0:T(4,128)(2,1)S(1)} all-to-all(bf16[4,4,4,1024]{3,2,1,0:T(4,128)(2,1)S(1)} %reshape.231), channel_id=1, replica_groups=mesh['dp'=4,'expert'=64] {'dp'}, dimensions={0} | all-to-all | bytes 262144 | tf_op jit(solution)/shard_map/all_to_all | solution.py:116
  (49 shorter events, 3.5 us)
Async XLA Ops:
  0.0 186.0 %copy-start = (bf16[1,4096,384]{2,1,0:T(8,128)(2,1)S(1)}, bf16[1,4096,384]{2,1,0:T(8,128)(2,1)}, u32[]{:S(2)}) copy-start(bf16[1,4096,384]{2,1,0:T(8,128)(2,1)} %param.15) | copy-start | bytes 9437188
  0.0 9.5 %copy-start.4 = (s32[16,4,8]{0,2,1:T(8,128)S(1)}, s32[16,4,8]{0,2,1:T(8,128)}, u32[]{:S(2)}) copy-start(s32[16,4,8]{0,2,1:T(8,128)} %param.10) | copy-start | bytes 6148
  0.0 10.3 %copy-start.5 = (s32[16]{0:T(128)S(1)}, s32[16]{0:T(128)}, u32[]{:S(2)}) copy-start(s32[16]{0:T(128)} %param.12) | copy-start | bytes 196
  3.7 20.9 %collective-permute-start.3 = (bf16[384,1024]{1,0:T(8,128)(2,1)}, bf16[384,1024]{1,0:T(8,128)(2,1)}, u32[]{:S(2)}, u32[]{:S(2)}) collective-permute-start(bf16[384,1024]{1,0:T(8,128)(2,1)} %get-tuple-element.16), channel_id=1, source_target_pairs={{0,64},{64,128},{128,192},{192,0},{1,65},{65,129},{129,193},{193,1... | collective-permute-start | bytes 2359304 | tf_op jit(solution)/shard_map/ppermute | solution.py:16
  5.3 37.3 %collective-permute-start.4 = (bf16[384,1024]{1,0:T(8,128)(2,1)}, bf16[384,1024]{1,0:T(8,128)(2,1)}, u32[]{:S(2)}, u32[]{:S(2)}) collective-permute-start(bf16[384,1024]{1,0:T(8,128)(2,1)} %get-tuple-element.18), channel_id=1, source_target_pairs={{0,128},{64,192},{128,0},{192,64},{1,129},{65,193},{129,1},{193,65... | collective-permute-start | bytes 2359304 | tf_op jit(solution)/shard_map/ppermute | solution.py:16
  8.2 34.4 %collective-permute-start.5 = (bf16[384,1024]{1,0:T(8,128)(2,1)}, bf16[384,1024]{1,0:T(8,128)(2,1)}, u32[]{:S(2)}, u32[]{:S(2)}) collective-permute-start(bf16[384,1024]{1,0:T(8,128)(2,1)} %get-tuple-element.15), channel_id=1, source_target_pairs={{0,192},{64,0},{128,64},{192,128},{1,193},{65,1},{129,65},{193,129... | collective-permute-start | bytes 2359304 | tf_op jit(solution)/shard_map/ppermute | solution.py:16
  45.2 40.9 %all-to-all-start.3 = ((bf16[64,2,4096]{2,1,0:T(2,128)(2,1)}), bf16[64,2,4096]{2,1,0:T(2,128)(2,1)}, u32[]{:S(2)}, u32[]{:S(2)}) async-start(bf16[64,2,4096]{2,1,0:T(2,128)(2,1)} %all_to_all.31), calls=%async_computation.3 | async-start | bytes 2097152 | tf_op jit(solution)/shard_map/all_to_all | solution.py:76
  86.1 34.6 %all-to-all-start = ((bf16[64,2,4096]{2,1,0:T(2,128)(2,1)}), bf16[64,2,4096]{2,1,0:T(2,128)(2,1)}, u32[]{:S(2)}, u32[]{:S(2)}) async-start(bf16[64,2,4096]{2,1,0:T(2,128)(2,1)} %all_to_all.27), calls=%async_computation | async-start | bytes 2097152 | tf_op jit(solution)/shard_map/all_to_all | solution.py:76
  124.3 53.1 %all-to-all-start.4 = ((bf16[4,128,4096]{2,1,0:T(8,128)(2,1)}), bf16[4,128,4096]{2,1,0:T(8,128)(2,1)}, u32[]{:S(2)}, u32[]{:S(2)}) async-start(bf16[4,128,4096]{2,1,0:T(8,128)(2,1)} %stack.76), calls=%async_computation.4 | async-start | bytes 8388608 | tf_op jit(solution)/shard_map/all_to_all | solution.py:78
  181.2 78.8 %all-to-all-start.1 = ((bf16[4,128,4096]{2,1,0:T(8,128)(2,1)}), bf16[4,128,4096]{2,1,0:T(8,128)(2,1)}, u32[]{:S(2)}, u32[]{:S(2)}) async-start(bf16[4,128,4096]{2,1,0:T(8,128)(2,1)} %stack.64), calls=%async_computation.1 | async-start | bytes 8388608 | tf_op jit(solution)/shard_map/all_to_all | solution.py:78
  186.0 4.7 %copy-start.6 = (bf16[1,4096,384]{2,1,0:T(8,128)(2,1)S(1)}, bf16[1,4096,384]{2,1,0:T(8,128)(2,1)}, u32[]{:S(2)}) copy-start(bf16[1,4096,384]{2,1,0:T(8,128)(2,1)} %param.16) | copy-start | bytes 9437188
  190.7 59.0 %copy-start.1 = (bf16[384,1024]{1,0:T(8,128)(2,1)S(1)}, bf16[384,1024]{1,0:T(8,128)(2,1)}, u32[]{:S(2)}) copy-start(bf16[384,1024]{1,0:T(8,128)(2,1)} %get-tuple-element.10) | copy-start | bytes 2359300
  195.4 47.9 %collective-permute-start.8 = (bf16[512,384]{1,0:T(8,128)(2,1)S(1)}, bf16[512,384]{1,0:T(8,128)(2,1)S(1)}, u32[]{:S(2)}, u32[]{:S(2)}) collective-permute-start(bf16[512,384]{1,0:T(8,128)(2,1)S(1)} %fusion.28), channel_id=1, source_target_pairs={{0,192},{64,0},{128,64},{192,128},{1,193},{65,1},{129,65},{193,129... | collective-permute-start | bytes 1179656 | tf_op jit(solution)/shard_map/ppermute | solution.py:24
  198.6 46.1 %collective-permute-start.7 = (bf16[512,384]{1,0:T(8,128)(2,1)S(1)}, bf16[512,384]{1,0:T(8,128)(2,1)S(1)}, u32[]{:S(2)}, u32[]{:S(2)}) collective-permute-start(bf16[512,384]{1,0:T(8,128)(2,1)S(1)} %fusion.28), channel_id=1, source_target_pairs={{0,128},{64,192},{128,0},{192,64},{1,129},{65,193},{129,1},{193,65... | collective-permute-start | bytes 1179656 | tf_op jit(solution)/shard_map/ppermute | solution.py:24
  199.5 50.2 %collective-permute-start.6 = (bf16[512,384]{1,0:T(8,128)(2,1)S(1)}, bf16[512,384]{1,0:T(8,128)(2,1)S(1)}, u32[]{:S(2)}, u32[]{:S(2)}) collective-permute-start(bf16[512,384]{1,0:T(8,128)(2,1)S(1)} %fusion.28), channel_id=1, source_target_pairs={{0,64},{64,128},{128,192},{192,0},{1,65},{65,129},{129,193},{193,1... | collective-permute-start | bytes 1179656 | tf_op jit(solution)/shard_map/ppermute | solution.py:24
  260.0 49.9 %all-to-all-start.5 = ((bf16[64,4,2,1024]{3,2,1,0:T(2,128)(2,1)}), bf16[64,4,2,1024]{3,2,1,0:T(2,128)(2,1)}, u32[]{:S(2)}, u32[]{:S(2)}) async-start(bf16[64,4,2,1024]{3,2,1,0:T(2,128)(2,1)} %bitcast.81), calls=%async_computation.5 | async-start | bytes 2097152 | tf_op jit(solution)/shard_map/all_to_all | solution.py:92
  268.0 4.7 %copy-start.7 = (bf16[1,4096,384]{2,1,0:T(8,128)(2,1)S(1)}, bf16[1,4096,384]{2,1,0:T(8,128)(2,1)}, u32[]{:S(2)}) copy-start(bf16[1,4096,384]{2,1,0:T(8,128)(2,1)} %param.16) | copy-start | bytes 9437188
  272.7 27.1 %copy-start.2 = (bf16[384,1024]{1,0:T(8,128)(2,1)S(1)}, bf16[384,1024]{1,0:T(8,128)(2,1)}, u32[]{:S(2)}) copy-start(bf16[384,1024]{1,0:T(8,128)(2,1)} %get-tuple-element.10) | copy-start | bytes 2359300
  277.4 12.0 %collective-permute-start.2 = (bf16[512,384]{1,0:T(8,128)(2,1)S(1)}, bf16[512,384]{1,0:T(8,128)(2,1)S(1)}, u32[]{:S(2)}, u32[]{:S(2)}) collective-permute-start(bf16[512,384]{1,0:T(8,128)(2,1)S(1)} %fusion.31), channel_id=1, source_target_pairs={{0,192},{64,0},{128,64},{192,128},{1,193},{65,1},{129,65},{193,129... | collective-permute-start | bytes 1179656 | tf_op jit(solution)/shard_map/ppermute | solution.py:24
  279.0 13.5 %collective-permute-start.1 = (bf16[512,384]{1,0:T(8,128)(2,1)S(1)}, bf16[512,384]{1,0:T(8,128)(2,1)S(1)}, u32[]{:S(2)}, u32[]{:S(2)}) collective-permute-start(bf16[512,384]{1,0:T(8,128)(2,1)S(1)} %fusion.31), channel_id=1, source_target_pairs={{0,128},{64,192},{128,0},{192,64},{1,129},{65,193},{129,1},{193,65... | collective-permute-start | bytes 1179656 | tf_op jit(solution)/shard_map/ppermute | solution.py:24
  280.4 19.4 %collective-permute-start = (bf16[512,384]{1,0:T(8,128)(2,1)S(1)}, bf16[512,384]{1,0:T(8,128)(2,1)S(1)}, u32[]{:S(2)}, u32[]{:S(2)}) collective-permute-start(bf16[512,384]{1,0:T(8,128)(2,1)S(1)} %fusion.31), channel_id=1, source_target_pairs={{0,64},{64,128},{128,192},{192,0},{1,65},{65,129},{129,193},{193,1... | collective-permute-start | bytes 1179656 | tf_op jit(solution)/shard_map/ppermute | solution.py:24
  304.2 16.1 %copy-start.3 = (f32[16,4,8]{0,2,1:T(8,128)S(1)}, f32[16,4,8]{0,2,1:T(8,128)}, u32[]{:S(2)}) copy-start(f32[16,4,8]{0,2,1:T(8,128)} %param.11) | copy-start | bytes 6148
  304.2 16.6 %copy-start.8 = (s32[16]{0:T(128)S(1)}, s32[16]{0:T(128)}, u32[]{:S(2)}) copy-start(s32[16]{0:T(128)} %param.14) | copy-start | bytes 196
  309.9 39.2 %all-to-all-start.2 = ((bf16[64,4,2,1024]{3,2,1,0:T(2,128)(2,1)}), bf16[64,4,2,1024]{3,2,1,0:T(2,128)(2,1)}, u32[]{:S(2)}, u32[]{:S(2)}) async-start(bf16[64,4,2,1024]{3,2,1,0:T(2,128)(2,1)} %bitcast.82), calls=%async_computation.2 | async-start | bytes 2097152 | tf_op jit(solution)/shard_map/all_to_all | solution.py:92
